TPU v7x, 256 devices: a whole 4x4x8 slice. The times are simulated.
256 devices in a mesh: row: 16 (over z_lo, y), col: 8 (over x, core), layer: 2 (over z_hi).
Axes of the slice: x: 4, y: 4, z: 8 (z_hi: 2, z_lo: 4; z = z_hi * 4 + z_lo), core: 2. Of those that a mesh axis runs over, the one named last changes fastest.
Arguments:
- density: float32 [2, 8192, 2048], P('layer', 'row', 'col'), may hold values from -6 to 6
- dens_mask: int32 [2, 128, 32], P('layer', 'row', 'col'), may hold values from 0 to 1, as said below
- hamiltonian: float32 [2, 2048, 16384], P('layer', 'row', 'col'), may hold values from -0.375 to 0.375
- ham_mask: int32 [2, 32, 256], P('layer', None, 'col'), may hold values from 0 to 1, as said below
- filter_mask: int32 [128, 256], P('row', 'col'), may hold values from 0 to 1, as said below
Outputs:
- product: float32 [8192, 16384], P('row', ('col', 'layer'))
Inputs may be any that keep to these rules, and one draw needn't show every extreme that they name: `dens_mask`: 1 where a density block is nonzero, else 0. `ham_mask`: 1 where a Hamiltonian block is nonzero, else 0. `filter_mask`: 1 where a result block is kept, else 0.
All inputs are finite; a program needn't handle non-finite values.
Results may differ from a plain program's by a relative error of at most 0.0001.
Values sent between devices are 32-bit elements; how exact they have to be, the bound alone decides.
No kernel may reach another device: no remote copies, remote signals or barrier semaphores. Data moves between devices by JAX's collectives and lax.ppermute only.
A program may use at most 128 MiB of HBM per device.

v0:
```python
import jax
import jax.numpy as jnp
from jax import lax
from jax.sharding import PartitionSpec as P

BLOCK = 64


def expand(block_mask):
    widened = jnp.repeat(block_mask.astype(jnp.float32), BLOCK, axis=-2)
    return jnp.repeat(widened, BLOCK, axis=-1)


def shards(density, dens_mask, hamiltonian, ham_mask, filter_mask):
    dens_vals = density * expand(dens_mask)
    ham_count = hamiltonian.shape[1]
    row_ids = lax.axis_index("row") * ham_count + jnp.arange(ham_count, dtype=jnp.int32)
    block_ids = row_ids // BLOCK
    one_hot = (
        block_ids[:, None] == jnp.arange(ham_mask.shape[1], dtype=jnp.int32)[None, :]
    ).astype(jnp.float32)
    picked = jnp.dot(
        one_hot,
        ham_mask[0].astype(jnp.float32),
        precision=lax.Precision.HIGHEST,
        preferred_element_type=jnp.float32,
    )
    ham_vals = hamiltonian * jnp.repeat(picked, BLOCK, axis=1)[None]
    kept = expand(filter_mask)
    ham_group = lax.all_gather(ham_vals, "row", axis=1, tiled=True)
    ham_part = ham_group[0]
    partial_value = jnp.dot(
        lax.all_gather(dens_vals, "col", axis=2, tiled=True)[0],
        ham_part,
        precision=lax.Precision.HIGHEST,
        preferred_element_type=jnp.float32,
    )
    return lax.psum_scatter(partial_value * kept, "layer", scatter_dimension=1, tiled=True)


def solution(mesh):
    return jax.shard_map(
        shards,
        mesh=mesh,
        in_specs=(
            P("layer", "row", "col"),
            P("layer", "row", "col"),
            P("layer", "row", "col"),
            P("layer", None, "col"),
            P("row", "col"),
        ),
        out_specs=P("row", ("col", "layer")),
        check_vma=False,
    )
```

profile of v0, /device:TPU:1, one launch (start us, length us, event | category | flops | bytes accessed | tf_op | source)
XLA Modules:
  0.0 426.2 jit_solution(16033029685912236478)
XLA Ops:
  6.5 0.0 copy-start.1
  6.5 0.0 copy-start
  6.5 0.0 all-gather.3.cloned.1.call-start
  6.5 1.3 copy.8
  7.8 0.7 convert_bitcast_fusion
  8.5 0.1 broadcast_in_dim.21
  8.6 0.1 broadcast_in_dim.22
  8.7 0.9 bitcast_multiply_fusion.1
  9.5 0.0 all-gather.3.cloned.1.call-update
  9.6 0.0 all-gather.5.cloned.1.call-start
  9.6 1.6 copy.9
  11.2 0.0 copy-done.1
  11.2 0.2 fusion.8
  11.4 1.1 bitcast_multiply_fusion
  12.5 0.0 all-gather.5.cloned.1.call-update
  12.5 0.0 reduce-scatter.2.cloned.1.call-start
  12.6 0.0 copy-done
  12.6 0.1 copy.10
  12.7 0.1 broadcast_in_dim.26
  12.8 0.1 reshape.35
  12.9 2.5 broadcast_in_dim.27
  15.4 5.5 %copy.11 = f32[512,2048]{1,0:T(8,128)} copy(f32[512,2048]{0,1:T(8,128)} %bitcast.24) | data formatting | bytes 8388608 | tf_op jit(solution)/shard_map/reshape | solution.py:11
  20.8 27.6 %all-gather.3.cloned.1.call-done = f32[1,512,2048]{1,2,0:T(8,128)} async-done(((f32[1,512,256]{1,2,0:T(8,128)}), f32[1,512,2048]{1,2,0:T(8,128)}) %all-gather.3.cloned.1.call-update) | async-done | bytes 4194320 | tf_op jit(solution)/shard_map/all_gather | solution.py:33
  48.5 194.2 %all-gather.5.cloned.1.call-done = f32[1,2048,2048]{1,2,0:T(8,128)} async-done(((f32[1,128,2048]{1,2,0:T(8,128)}), f32[1,2048,2048]{1,2,0:T(8,128)}) %all-gather.5.cloned.1.call-update) | async-done | bytes 16777232 | tf_op jit(solution)/shard_map/all_gather | solution.py:30
  242.7 57.7 %fusion.3 = f32[512,2048]{1,0:T(8,128)} fusion(f32[512,2048]{1,0:T(8,128)} %copy.11, f32[1,2048,2048]{1,2,0:T(8,128)} %all-gather.5.cloned.1.call-done, f32[1,512,2048]{1,2,0:T(8,128)} %all-gather.3.cloned.1.call-done), kind=kOutput, calls=%fused_computation.3 | convolution fusion | flops 25770852352 | bytes 29360128 | tf_op jit(solution)/shard_map/dot_general | solution.py:32
  300.3 0.0 reduce-scatter.2.cloned.1.call-update
  300.3 119.4 %reduce-scatter.2.cloned.1.call-done = f32[512,1024]{1,0:T(8,128)} async-done(((f32[512,2048]{1,0:T(8,128)}), f32[512,1024]{1,0:T(8,128)}) %reduce-scatter.2.cloned.1.call-update) | async-done | bytes 2097168 | tf_op jit(solution)/shard_map/reduce_scatter | solution.py:38
  (2 shorter events, 0.0 us)
Async XLA Ops:
  6.5 4.7 %copy-start.1 = (s32[1,32,32]{2,1,0:T(8,128)S(1)}, s32[1,32,32]{2,1,0:T(8,128)}, u32[]{:S(2)}) copy-start(s32[1,32,32]{2,1,0:T(8,128)} %param.8) | copy-start | bytes 12292
  6.5 6.1 %copy-start = (s32[8,32]{1,0:T(8,128)S(1)}, s32[8,32]{1,0:T(8,128)}, u32[]{:S(2)}) copy-start(s32[8,32]{1,0:T(8,128)} %param.9) | copy-start | bytes 3076
  6.5 41.9 %all-gather.3.cloned.1.call-start = ((), (), s32[]{:S(2)}) async-start(), calls=%async_computation.1 | async-start | bytes 4718592 | tf_op jit(solution)/shard_map/all_gather | solution.py:33
  9.6 233.1 %all-gather.5.cloned.1.call-start = ((), (), s32[]{:S(2)}) async-start(), calls=%async_computation.2 | async-start | bytes 17825792 | tf_op jit(solution)/shard_map/all_gather | solution.py:30
  12.5 407.2 %reduce-scatter.2.cloned.1.call-start = ((), (), s32[]{:S(2)}) async-start(), calls=%async_computation.3 | async-start | bytes 6291456 | tf_op jit(solution)/shard_map/reduce_scatter | solution.py:38
Sparse Core Ops, SparseCore 0:
  9.7 38.7 all-gather.2
  50.2 192.4 all-gather.4
  300.5 119.2 reduce-scatter.1
where the time goes:
time: 426 us
  waiting for transfers between devices  341 us (80%)
  matrix products  57.9 us (14%)
  between operations  13.2 us (3%)
  local copies, waits for them, and re-layouts  11.2 us (3%)
    all_gather x1, waiting for transfers between devices, shards(): ham_group = lax.all_gather(ham_vals, 'row', axis=1, tiled=True)  194 us
    reduce_scatter x1, waiting for transfers between devices, shards(): lax.psum_scatter(partial_value * kept, 'layer', scatter_dimension=1, tile...  119 us
    dot_general x1, matrix products, shards(): jnp.dot(lax.all_gather(dens_vals, 'col', axis=2, tiled=True)[0], ham_part...  57.7 us
    all_gather x1, waiting for transfers between devices, shards(): lax.all_gather(dens_vals, 'col', axis=2, tiled=True)[0]  27.6 us
  transfers between devices with their start and end apart: 3, of which 3 were waited for; matrix products, arithmetic and copies ran while one was open for 3% of the time, Pallas kernels for 0%

commit v1 on v0

--- a/solution.py
+++ b/solution.py
@@ -4,6 +4,22 @@
 from jax.sharding import PartitionSpec as P
 
 BLOCK = 64
+
+
+def collect(x, axis, dim):
+    ways, here, lap = (lax.axis_size(axis), lax.axis_index(axis), x.shape[dim])
+    shape = [n * ways if d == dim else n for d, n in enumerate(x.shape)]
+    full = lax.dynamic_update_slice_in_dim(jnp.zeros(shape, x.dtype), x, here * lap, axis=dim)
+    going_up = going_down = x
+    for far in range(1, ways // 2 + 1):
+        going_up = lax.ppermute(going_up, axis, [(d, (d + 1) % ways) for d in range(ways)])
+        full = lax.dynamic_update_slice_in_dim(full, going_up, (here - far) % ways * lap, axis=dim)
+        if 2 * far < ways:
+            going_down = lax.ppermute(going_down, axis, [(d, (d - 1) % ways) for d in range(ways)])
+            full = lax.dynamic_update_slice_in_dim(
+                full, going_down, (here + far) % ways * lap, axis=dim
+            )
+    return full
 
 
 def expand(block_mask):
@@ -30,7 +46,7 @@
     ham_group = lax.all_gather(ham_vals, "row", axis=1, tiled=True)
     ham_part = ham_group[0]
     partial_value = jnp.dot(
-        lax.all_gather(dens_vals, "col", axis=2, tiled=True)[0],
+        collect(dens_vals, "col", 2)[0],
         ham_part,
         precision=lax.Precision.HIGHEST,
         preferred_element_type=jnp.float32,

time: 426 us -> 391 us (0.918)
  waiting for transfers between devices: 341 us -> 286 us
  starting transfers between devices: 0.09 us -> 12.7 us
  local copies, waits for them, and re-layouts: 11.2 us -> 18.5 us
    all_gather x1, waiting for transfers between devices: 194 us -> 156 us  [shards(): ham_group = lax.all_gather(ham_vals, 'row', axis=1, tiled=True)]
    all_gather x1 -> x0, waiting for transfers between devices: 27.6 us -> none  [shards(): lax.all_gather(dens_vals, 'col', axis=2, tiled=True)[0]]
    ppermute x0 -> x7, starting transfers between devices: none -> 12.6 us  [the longest x4 7.72 us: collect(): lax.ppermute(going_up, axis, [(d, (d + 1) % ways) for d in range(ways)])]
    ppermute x0 -> x7, waiting for transfers between devices: none -> 10.3 us  [the longest x4 9.55 us: collect(): lax.ppermute(going_up, axis, [(d, (d + 1) % ways) for d in range(ways)])]
    dynamic_update_slice x0 -> x7, local copies, waits for them, and re-layouts: none -> 5.85 us  [the longest x4 3.35 us: collect(): lax.dynamic_update_slice_in_dim(full, going_up, (here - far) % ways * lap...]
  transfers between devices with their start and end apart: 3 -> 9, of which waited for: 3 -> 7; matrix products, arithmetic and copies ran while one was open for 3% -> 5% of each run, Pallas kernels for 0% -> 0%
where the time goes in v1:
time: 391 us
  waiting for transfers between devices  286 us (73%)
  matrix products  58.5 us (15%)
  local copies, waits for them, and re-layouts  18.5 us (5%)
  between operations  13.5 us (3%)
  starting transfers between devices  12.7 us (3%)
    all_gather x1, waiting for transfers between devices, shards(): ham_group = lax.all_gather(ham_vals, 'row', axis=1, tiled=True)  156 us
    reduce_scatter x1, waiting for transfers between devices, shards(): lax.psum_scatter(partial_value * kept, 'layer', scatter_dimension=1, tile...  119 us
    dot_general x1, matrix products, shards(): jnp.dot(collect(dens_vals, 'col', 2)[0], ham_part, precision=lax.Precisio...  57.6 us
    ppermute x4, waiting for transfers between devices, collect(): lax.ppermute(going_up, axis, [(d, (d + 1) % ways) for d in range(ways)])  9.55 us
  transfers between devices with their start and end apart: 9, of which 7 were waited for; matrix products, arithmetic and copies ran while one was open for 5% of the time, Pallas kernels for 0%

profile of v1, /device:TPU:1, one launch (start us, length us, event | category | flops | bytes accessed | tf_op | source)
XLA Modules:
  0.0 390.8 jit_solution(5727720032576247118)
XLA Ops:
  6.5 1.6 copy.9
  8.2 0.9 fusion.5
  9.1 1.1 bitcast_multiply_fusion
  10.3 0.2 copy.8
  10.7 2.5 squeeze.23
  13.2 1.0 bitcast_dynamic-update-slice_fusion.7
  14.1 2.6 collective-permute-start
  16.7 0.6 collective-permute-start.1
  17.3 5.5 %collective-permute-done = f32[1,512,256]{1,2,0:T(8,128)S(1)} collective-permute-done((f32[1,512,256]{1,2,0:T(8,128)S(1)}, f32[1,512,256]{1,2,0:T(8,128)S(1)}, u32[]{:S(2)}, u32[]{:S(2)}) %collective-permute-start) | collective-permute-done | bytes 524320 | tf_op jit(solution)/shard_map/ppermute | solution.py:15
  22.8 2.5 collective-permute-start.2
  25.3 0.3 collective-permute-done.1
  25.6 1.6 collective-permute-start.3
  27.2 0.1 broadcast_in_dim.27
  27.3 0.1 reshape.51
  27.4 2.5 broadcast_in_dim.28
  29.9 5.4 %copy.11 = f32[512,2048]{1,0:T(8,128)} copy(f32[512,2048]{0,1:T(8,128)} %bitcast.36) | data formatting | bytes 8388608 | tf_op jit(solution)/shard_map/reshape | solution.py:27
  35.3 0.2 collective-permute-start.4
  35.5 0.9 bitcast_dynamic-update-slice_fusion.6
  36.4 0.8 bitcast_dynamic-update-slice_fusion.5
  37.2 2.7 collective-permute-start.5
  40.0 0.8 bitcast_dynamic-update-slice_fusion.4
  40.8 0.9 collective-permute-done.4
  41.7 2.5 collective-permute-start.6
  44.1 0.8 bitcast_dynamic-update-slice_fusion.3
  45.0 0.8 bitcast_dynamic-update-slice_fusion.2
  45.8 0.4 collective-permute-done.5
  46.2 0.8 bitcast_dynamic-update-slice_fusion.1
  47.1 3.2 collective-permute-done.6
  50.3 0.8 bitcast_dynamic-update-slice_fusion
  51.1 155.9 %all-gather.2.cloned.1.call-done = f32[1,2048,2048]{1,2,0:T(8,128)} async-done(((f32[1,128,2048]{1,2,0:T(8,128)}), f32[1,2048,2048]{1,2,0:T(8,128)}) %all-gather.2.cloned.1.call-update) | async-done | bytes 16777232 | tf_op jit(solution)/shard_map/all_gather | solution.py:46
  207.0 57.6 %fusion.2 = f32[512,2048]{1,0:T(8,128)} fusion(f32[512,2048]{1,0:T(8,128)} %copy.11, f32[512,2048]{0,1:T(8,128)} %bitcast_dynamic-update-slice_fusion, f32[1,2048,2048]{1,2,0:T(8,128)} %all-gather.2.cloned.1.call-done), kind=kOutput, calls=%fused_computation.2 | convolution fusion | flops 25770852352 | bytes 29360128 | tf_op jit(solution)/shard_map/dot_general | solution.py:48
  264.6 119.4 %reduce-scatter.2.cloned.1.call-done = f32[512,1024]{1,0:T(8,128)} async-done(((f32[512,2048]{1,0:T(8,128)}), f32[512,1024]{1,0:T(8,128)}) %reduce-scatter.2.cloned.1.call-update) | async-done | bytes 2097168 | tf_op jit(solution)/shard_map/reduce_scatter | solution.py:54
  (18 shorter events, 0.3 us)
Async XLA Ops:
  6.5 3.7 copy-start
  6.5 4.0 %copy-start.2 = (s32[1,8,4]{1,2,0:T(4,128)S(1)}, s32[1,8,4]{1,2,0:T(4,128)}, u32[]{:S(2)}) copy-start(s32[1,8,4]{1,2,0:T(4,128)} %param.6) | copy-start | bytes 388
  6.5 200.5 %all-gather.2.cloned.1.call-start = ((), (), s32[]{:S(2)}) async-start(), calls=%async_computation.1 | async-start | bytes 17825792 | tf_op jit(solution)/shard_map/all_gather | solution.py:46
  10.2 16.9 %copy-start.1 = (s32[8,32]{1,0:T(8,128)S(1)}, s32[8,32]{1,0:T(8,128)}, u32[]{:S(2)}) copy-start(s32[8,32]{1,0:T(8,128)} %param.9) | copy-start | bytes 3076
  10.2 373.7 %reduce-scatter.2.cloned.1.call-start = ((), (), s32[]{:S(2)}) async-start(), calls=%async_computation.2 | async-start | bytes 6291456 | tf_op jit(solution)/shard_map/reduce_scatter | solution.py:54
  14.1 8.7 %collective-permute-start = (f32[1,512,256]{1,2,0:T(8,128)S(1)}, f32[1,512,256]{1,2,0:T(8,128)S(1)}, u32[]{:S(2)}, u32[]{:S(2)}) collective-permute-start(f32[1,512,256]{1,2,0:T(8,128)S(1)} %get-tuple-element.6), channel_id=1, source_target_pairs={{0,2},{2,4},{4,6},{6,8},{8,10},{10,12},{12,14},{14,0},{1,3},{3,5},... | collective-permute-start | bytes 1572872 | tf_op jit(solution)/shard_map/ppermute | solution.py:15
  16.7 8.9 %collective-permute-start.1 = (f32[1,512,256]{1,2,0:T(8,128)S(1)}, f32[1,512,256]{1,2,0:T(8,128)S(1)}, u32[]{:S(2)}, u32[]{:S(2)}) collective-permute-start(f32[1,512,256]{1,2,0:T(8,128)S(1)} %get-tuple-element.6), channel_id=1, source_target_pairs={{0,14},{2,0},{4,2},{6,4},{8,6},{10,8},{12,10},{14,12},{1,15},{3,1}... | collective-permute-start | bytes 1572872 | tf_op jit(solution)/shard_map/ppermute | solution.py:18
  22.8 12.5 %collective-permute-start.2 = (f32[1,512,256]{1,2,0:T(8,128)S(1)}, f32[1,512,256]{1,2,0:T(8,128)S(1)}, u32[]{:S(2)}, u32[]{:S(2)}) collective-permute-start(f32[1,512,256]{1,2,0:T(8,128)S(1)} %collective-permute-done), channel_id=1, source_target_pairs={{0,2},{2,4},{4,6},{6,8},{8,10},{10,12},{12,14},{14,0},{1,3},{3,5},... | collective-permute-start | bytes 1572872 | tf_op jit(solution)/shard_map/ppermute | solution.py:15
  25.6 11.6 %collective-permute-start.3 = (f32[1,512,256]{1,2,0:T(8,128)S(1)}, f32[1,512,256]{1,2,0:T(8,128)S(1)}, u32[]{:S(2)}, u32[]{:S(2)}) collective-permute-start(f32[1,512,256]{1,2,0:T(8,128)S(1)} %collective-permute-done.1), channel_id=1, source_target_pairs={{0,14},{2,0},{4,2},{6,4},{8,6},{10,8},{12,10},{14,12},{1,15},{3,1}... | collective-permute-start | bytes 1572872 | tf_op jit(solution)/shard_map/ppermute | solution.py:18
  35.3 6.3 %collective-permute-start.4 = (f32[1,512,256]{1,2,0:T(8,128)S(1)}, f32[1,512,256]{1,2,0:T(8,128)S(1)}, u32[]{:S(2)}, u32[]{:S(2)}) collective-permute-start(f32[1,512,256]{1,2,0:T(8,128)S(1)} %collective-permute-done.2), channel_id=1, source_target_pairs={{0,2},{2,4},{4,6},{6,8},{8,10},{10,12},{12,14},{14,0},{1,3},{3,5},... | collective-permute-start | bytes 1572872 | tf_op jit(solution)/shard_map/ppermute | solution.py:15
  37.2 9.0 %collective-permute-start.5 = (f32[1,512,256]{1,2,0:T(8,128)S(1)}, f32[1,512,256]{1,2,0:T(8,128)S(1)}, u32[]{:S(2)}, u32[]{:S(2)}) collective-permute-start(f32[1,512,256]{1,2,0:T(8,128)S(1)} %collective-permute-done.3), channel_id=1, source_target_pairs={{0,14},{2,0},{4,2},{6,4},{8,6},{10,8},{12,10},{14,12},{1,15},{3,1}... | collective-permute-start | bytes 1572872 | tf_op jit(solution)/shard_map/ppermute | solution.py:18
  41.7 8.6 %collective-permute-start.6 = (f32[1,512,256]{1,2,0:T(8,128)S(1)}, f32[1,512,256]{1,2,0:T(8,128)S(1)}, u32[]{:S(2)}, u32[]{:S(2)}) collective-permute-start(f32[1,512,256]{1,2,0:T(8,128)S(1)} %collective-permute-done.4), channel_id=1, source_target_pairs={{0,2},{2,4},{4,6},{6,8},{8,10},{10,12},{12,14},{14,0},{1,3},{3,5},... | collective-permute-start | bytes 1572872 | tf_op jit(solution)/shard_map/ppermute | solution.py:15
Sparse Core Ops, SparseCore 0:
  10.3 196.6 all-gather.1
  264.7 119.2 reduce-scatter.1
